TPU v7x, 32 devices: a whole 2x2x4 slice. The times are simulated.
32 devices in a mesh: ctx: 16 (over z, y, core), head: 2 (over x).
Axes of the slice: x: 2, y: 2, z: 4, core: 2. Of those that a mesh axis runs over, the one named last changes fastest.
Arguments:
- queries: bfloat16 [2048, 1536], P('ctx', 'head'), may hold values from -45 to 45
- key_rows: bfloat16 [2048, 256], P('ctx', 'head'), may hold values from -5 to 5
- value_rows: bfloat16 [2048, 256], P('ctx', 'head'), may hold values from -18 to 18
- cotangent: bfloat16 [2048, 1536], P('ctx', 'head'), may hold values from -6 to 6
- trace_ids: int32 [2048], P('ctx'), may hold values from 0 to 15, never falling along the last dimension, each value on 1 to 512 neighbouring positions
- correct: int32 [16], replicated, may hold values from 0 to 16, as said below
- group_size: int32 [16], replicated, may hold values from 4 to 16
Outputs:
- log_totals: float32 [2048, 12], P('ctx', 'head')
- grad_queries: float32 [2048, 1536], P('ctx', 'head')
- grad_keys: bfloat16 [2048, 256], P('ctx', 'head')
- grad_values: bfloat16 [2048, 256], P('ctx', 'head')
Inputs may be any that keep to these rules, and one draw needn't show every extreme that they name: correct[g] is at most group_size[g].
All inputs are finite; a program needn't handle non-finite values.
Results may differ from a plain program's by a relative error of at most 0.0054.
Values may be sent and summed in bfloat16 or wider, within the bound.
No kernel may reach another device: no remote copies, remote signals or barrier semaphores. Data moves between devices by JAX's collectives and lax.ppermute only.
A program may use at most 64 MiB of HBM per device.

v0:
```python
import math
import jax
import jax.numpy as jnp
from jax import lax
from jax.sharding import PartitionSpec as P

PASSK = 4


def pass_rate(correct, group_size):
    counts = group_size.astype(jnp.float32)
    hit_counts = correct.astype(jnp.float32)
    product = jnp.ones_like(counts)
    for offset in range(PASSK):
        product = product * (counts - hit_counts - offset) / (counts - offset)
    return 1.0 - product


def body(queries, key_rows, value_rows, cotangent, trace_ids, correct, group_size):
    tok_rows = queries.shape[0]
    half_rows = tok_rows // 2
    row_width = queries.shape[1]
    head_dim = key_rows.shape[1]
    head_count = row_width // head_dim
    ctx_count = lax.axis_size("ctx")
    my_index = lax.axis_index("ctx")
    length = tok_rows * ctx_count
    score_scale = 1.0 / math.sqrt(head_dim)
    pass_rates = pass_rate(correct, group_size)
    traces = jnp.arange(pass_rates.shape[0], dtype=jnp.int32)
    weights = jnp.sum(
        jnp.where(trace_ids[:, None] == traces[None, :], pass_rates[None, :], 0.0), axis=1
    )
    out_grads = (weights[:, None] * cotangent.astype(jnp.float32)).astype(jnp.bfloat16)
    first_base = my_index * tok_rows
    second_base = first_base + half_rows
    local_pos = jnp.arange(half_rows, dtype=jnp.int32)
    positions = jnp.concatenate([first_base + local_pos, second_base + local_pos], 0)
    last_first = first_base + half_rows - 1
    last_second = second_base + half_rows - 1
    query_all = queries.reshape(tok_rows, head_count, head_dim)
    grad_all = out_grads.reshape(tok_rows, head_count, head_dim)

    def run_block(running, key_block, value_block, key_start, block_fn):
        need_first = (key_start <= last_first).astype(jnp.int32)
        need_second = (key_start <= last_second).astype(jnp.int32)
        branch_index = need_first + 2 * need_second

        def skip_block(values_in):
            return values_in

        def first_only(values_in):
            return block_fn((0, half_rows), values_in, key_block, value_block, key_start)

        def second_only(values_in):
            return block_fn((half_rows, tok_rows), values_in, key_block, value_block, key_start)

        def both_halves(values_in):
            return block_fn((0, tok_rows), values_in, key_block, value_block, key_start)

        return lax.switch(branch_index, [skip_block, first_only, second_only, both_halves], running)

    def forward_block(row_span, running, key_block, value_block, key_start):
        row_begin, row_end = row_span
        row_peak, row_total, weighted = running
        query_part = query_all[row_begin:row_end]
        grad_part = grad_all[row_begin:row_end]
        query_pos = positions[row_begin:row_end]
        scores = (
            jnp.einsum("tqd,kd->tqk", query_part, key_block, preferred_element_type=jnp.float32)
            * score_scale
        )
        key_pos = key_start + jnp.arange(key_block.shape[0], dtype=jnp.int32)
        visible = key_pos[None, None, :] <= query_pos[:, None, None]
        block_peak = jnp.max(jnp.where(visible, scores, -1e30), axis=2)
        old_peak = row_peak[row_begin:row_end]
        new_peak = jnp.maximum(old_peak, block_peak)
        exp_terms = jnp.where(visible, jnp.exp(scores - new_peak[:, :, None]), 0.0)
        grad_probs = jnp.einsum(
            "tqd,kd->tqk", grad_part, value_block, preferred_element_type=jnp.float32
        )
        shrink = jnp.exp(old_peak - new_peak)
        new_total = row_total[row_begin:row_end] * shrink + jnp.sum(exp_terms, axis=2)
        new_weighted = weighted[row_begin:row_end] * shrink + jnp.sum(
            exp_terms * grad_probs, axis=2
        )
        return (
            row_peak.at[row_begin:row_end].set(new_peak),
            row_total.at[row_begin:row_end].set(new_total),
            weighted.at[row_begin:row_end].set(new_weighted),
        )

    row_peak = jnp.full((tok_rows, head_count), -1e30, jnp.float32)
    row_total = jnp.zeros((tok_rows, head_count), jnp.float32)
    weighted = jnp.zeros((tok_rows, head_count), jnp.float32)
    key_piece = lax.all_gather(key_rows, "ctx", axis=0, tiled=True)
    value_piece = lax.all_gather(value_rows, "ctx", axis=0, tiled=True)
    piece_rows = key_piece.shape[0]
    block_rows = math.gcd(piece_rows, 512)

    def forward_step(step_index, statistics):
        offset = step_index * block_rows
        key_block = lax.dynamic_slice_in_dim(key_piece, offset, block_rows, 0)
        value_block = lax.dynamic_slice_in_dim(value_piece, offset, block_rows, 0)
        return run_block(statistics, key_block, value_block, offset, forward_block)

    statistics = lax.fori_loop(
        0, piece_rows // block_rows, forward_step, (row_peak, row_total, weighted)
    )
    folded = statistics + (key_piece, value_piece)
    row_peak, row_total, weighted, key_store, value_store = folded
    log_totals = row_peak + jnp.log(row_total)
    delta_rows = weighted / row_total

    def backward_block(row_span, running, key_block, value_block, key_start):
        row_begin, row_end = row_span
        grad_query, zero_block = running
        query_part = query_all[row_begin:row_end]
        grad_part = grad_all[row_begin:row_end]
        query_pos = positions[row_begin:row_end]
        scores = (
            jnp.einsum("tqd,kd->tqk", query_part, key_block, preferred_element_type=jnp.float32)
            * score_scale
        )
        key_pos = key_start + jnp.arange(key_block.shape[0], dtype=jnp.int32)
        visible = key_pos[None, None, :] <= query_pos[:, None, None]
        probabilities = jnp.where(
            visible, jnp.exp(scores - log_totals[row_begin:row_end][:, :, None]), 0.0
        )
        prob_bf16 = probabilities.astype(jnp.bfloat16)
        grad_probs = jnp.einsum(
            "tqd,kd->tqk", grad_part, value_block, preferred_element_type=jnp.float32
        )
        grad_scores = (
            probabilities * (grad_probs - delta_rows[row_begin:row_end][:, :, None])
        ).astype(jnp.bfloat16)
        query_add = (
            jnp.einsum("tqk,kd->tqd", grad_scores, key_block, preferred_element_type=jnp.float32)
            * score_scale
        )
        key_add = (
            jnp.einsum("tqk,tqd->kd", grad_scores, query_part, preferred_element_type=jnp.float32)
            * score_scale
        )
        value_add = jnp.einsum(
            "tqk,tqd->kd", prob_bf16, grad_part, preferred_element_type=jnp.float32
        )
        return (
            grad_query.at[row_begin:row_end].add(query_add),
            jnp.concatenate([key_add, value_add], 1),
        )

    query_zero = jnp.zeros((tok_rows, head_count, head_dim), jnp.float32)
    key_block_rows = math.gcd(length, 512)

    def backward_step(step_index, running):
        grad_query, partial_sums = running
        key_start = step_index * key_block_rows
        key_block = lax.dynamic_slice_in_dim(key_store, key_start, key_block_rows, 0)
        value_block = lax.dynamic_slice_in_dim(value_store, key_start, key_block_rows, 0)
        zero_block = jnp.zeros((key_block_rows, 2 * head_dim), jnp.float32)
        grad_query, block_sums = run_block(
            (grad_query, zero_block), key_block, value_block, key_start, backward_block
        )
        partial_sums = lax.dynamic_update_slice_in_dim(partial_sums, block_sums, key_start, 0)
        return (grad_query, partial_sums)

    grad_query, partial_sums = lax.fori_loop(
        0,
        length // key_block_rows,
        backward_step,
        (query_zero, jnp.zeros((length, 2 * head_dim), jnp.float32)),
    )
    reduced = jnp.sum(
        lax.all_to_all(
            partial_sums.reshape(ctx_count, tok_rows, 2 * head_dim),
            "ctx",
            split_axis=0,
            concat_axis=0,
            tiled=True,
        ),
        axis=0,
    )
    grad_keys = reduced[:, :head_dim].astype(jnp.bfloat16)
    grad_values = reduced[:, head_dim:].astype(jnp.bfloat16)
    query_grads = grad_query.reshape(tok_rows, row_width)
    return (log_totals, query_grads, grad_keys, grad_values)


def solution(mesh):
    return jax.shard_map(
        body,
        mesh=mesh,
        in_specs=(
            P("ctx", "head"),
            P("ctx", "head"),
            P("ctx", "head"),
            P("ctx", "head"),
            P("ctx"),
            P(),
            P(),
        ),
        out_specs=(P("ctx", "head"), P("ctx", "head"), P("ctx", "head"), P("ctx", "head")),
        check_vma=False,
    )
```

profile of v0, /device:TPU:13, one launch (start us, length us, event | category | flops | bytes accessed | tf_op | source)
XLA Modules:
  0.0 124.0 jit_solution(4631487437105801853)
XLA Ops:
  0.7 0.7 fusion.61
  1.4 0.7 select_reduce_fusion.3
  2.1 1.0 multiply_convert_fusion.1
  3.1 0.2 copy.73
  3.3 0.2 copy.75
  3.5 1.1 copy.72
  4.6 0.2 copy.74
  4.8 17.1 %all_gather.6 = bf16[2048,128]{1,0:T(8,128)(2,1)S(1)} all-gather(bf16[128,128]{1,0:T(8,128)(2,1)S(1)} %copy-done.1), channel_id=1, replica_groups=mesh['ctx'=16,'head'=2] {'ctx'}, dimensions={0}, use_global_device_ids=true | all-gather | bytes 557056 | tf_op jit(solution)/shard_map/all_gather | solution.py:96
  21.9 22.8 %all_gather.7 = bf16[2048,128]{1,0:T(8,128)(2,1)S(1)} all-gather(bf16[128,128]{1,0:T(8,128)(2,1)S(1)} %copy-done.2), channel_id=1, replica_groups=mesh['ctx'=16,'head'=2] {'ctx'}, dimensions={0}, use_global_device_ids=true | all-gather | bytes 557056 | tf_op jit(solution)/shard_map/all_gather | solution.py:97
  44.8 3.9 %while.53 = (s32[]{:T(128)}, f32[128,6]{0,1:T(8,128)S(1)}, f32[128,6]{0,1:T(8,128)S(1)}, f32[128,6]{0,1:T(8,128)S(1)}, s32[]{:T(128)}, /*index=5*/s32[]{:T(128)}...) while((s32[]{:T(128)}, f32[128,6]{0,1:T(8,128)S(1)}, ...), condition=%wide.region_15.0_spmd.clone, body=%wide.region_1.15_spmd.clone.sunk | while | flops 205327120 | bytes 6221379 | solution.py:107
  44.8 1.7 %conditional.6 = ((f32[128,6]{0,1:T(8,128)S(1)}, f32[128,6]{0,1:T(8,128)S(1)}, f32[128,6]{0,1:T(8,128)S(1)})) conditional(s32[]{:T(128)} %clamp.18, (f32[128,6]{0,1:T(8,128)S(1)}, f32[128,6]{0,1:T(8,128)S(1)}, f32[128,6]{0,1:T(8,128)S(1)}) %tuple.202, (f32[128,6]{0,1:T(8,128)S(1)}, s32[]{:T(128)}, s32[]{:T(128)}, ...), branch_computations={%region_2.2_spmd, %region_3.6_spmd, %region_7.10_spmd, %region_11.... | conditional | flops 205327104 | bytes 5696036 | solution.py:61
  44.9 0.1 broadcast_compare_fusion.2
  45.0 0.5 select_reduce_fusion.2
  45.4 0.6 multiply_reduce_fusion
  46.0 0.5 fusion.20
  46.6 1.7 %conditional.6 = ((f32[128,6]{0,1:T(8,128)S(1)}, f32[128,6]{0,1:T(8,128)S(1)}, f32[128,6]{0,1:T(8,128)S(1)})) conditional(s32[]{:T(128)} %clamp.18, (f32[128,6]{0,1:T(8,128)S(1)}, f32[128,6]{0,1:T(8,128)S(1)}, f32[128,6]{0,1:T(8,128)S(1)}) %tuple.202, (f32[128,6]{0,1:T(8,128)S(1)}, s32[]{:T(128)}, s32[]{:T(128)}, ...), branch_computations={%region_2.2_spmd, %region_3.6_spmd, %region_7.10_spmd, %region_11.... | conditional | flops 205327104 | bytes 5696036 | solution.py:61
  46.8 0.5 select_reduce_fusion.2
  47.3 0.6 multiply_reduce_fusion
  47.8 0.5 fusion.20
  48.7 1.5 %broadcast_in_dim.124.clone = f32[2048,256]{1,0:T(8,128)} broadcast(f32[]{:T(128)} %constant.488.clone.1), dimensions={} | broadcast | bytes 2097156 | tf_op jit(solution)/shard_map/broadcast_in_dim | solution.py:172
  50.2 8.7 %while.54 = (s32[]{:T(128)}, f32[128,6,128]{2,0,1:T(8,128)S(1)}, f32[2048,256]{1,0:T(8,128)}, s32[]{:T(128)}, s32[]{:T(128)}, /*index=5*/bf16[2048,128]{1,0:T(8,...) while((s32[]{:T(128)}, f32[128,6,128]{2,0,1:T(8,128)S(1)}, ...), condition=%wide.region_21.22_spmd.clone, body=%wide.region_16.21_spmd.clone.sunk | while | flops 506528256 | bytes 13381159 | solution.py:168
  50.2 2.1 %conditional.7 = (f32[128,6,128]{2,0,1:T(8,128)S(1)}, f32[512,256]{0,1:T(8,128)S(1)}) conditional(s32[]{:T(128)} %clamp.19, f32[128,6,128]{2,0,1:T(8,128)S(1)} %get-tuple-element.1421, (f32[128,6,128]{2,0,1:T(8,128)S(1)}, s32[]{:T(128)}, s32[]{:T(128)}, bf16[128,6,128]{0,2,1:T(8,128)(2,1)S(1)}, ...), branch_computations={%region_17.17_spmd, %region_18.18_spmd, %region_19.19_spmd, %regio... | conditional | flops 506528256 | bytes 10758676 | solution.py:61
  50.4 0.5 exponential_select_fusion.3
  50.9 0.3 convolution_bitcast_fusion.4
  51.2 0.4 multiply_convert_fusion
  51.6 0.3 fusion.56
  51.9 0.4 fusion.55
  52.3 0.2 copy.91
  52.5 0.8 constant_dynamic-update-slice_fusion.2
  53.4 2.1 %conditional.7 = (f32[128,6,128]{2,0,1:T(8,128)S(1)}, f32[512,256]{0,1:T(8,128)S(1)}) conditional(s32[]{:T(128)} %clamp.19, f32[128,6,128]{2,0,1:T(8,128)S(1)} %get-tuple-element.1421, (f32[128,6,128]{2,0,1:T(8,128)S(1)}, s32[]{:T(128)}, s32[]{:T(128)}, bf16[128,6,128]{0,2,1:T(8,128)(2,1)S(1)}, ...), branch_computations={%region_17.17_spmd, %region_18.18_spmd, %region_19.19_spmd, %regio... | conditional | flops 506528256 | bytes 10758676 | solution.py:61
  53.5 0.5 exponential_select_fusion.3
  54.1 0.3 convolution_bitcast_fusion.4
  54.3 0.4 multiply_convert_fusion
  54.8 0.3 fusion.56
  55.0 0.4 fusion.55
  55.5 0.2 copy.91
  55.7 0.9 constant_dynamic-update-slice_fusion.2
  56.7 0.2 copy.91
  56.9 0.9 constant_dynamic-update-slice_fusion.2
  57.8 0.2 copy.91
  58.1 0.9 constant_dynamic-update-slice_fusion.2
  58.9 2.9 %copy.78 = f32[16,128,256]{1,2,0:T(8,128)} copy(f32[16,128,256]{2,1,0:T(8,128)} %bitcast.88) | data formatting | bytes 4194304 | tf_op jit(solution)/shard_map/reshape | solution.py:176
  61.8 13.2 %all-to-all-start = ((f32[16,128,256]{1,2,0:T(8,128)}), f32[16,128,256]{1,2,0:T(8,128)S(1)}, u32[]{:S(2)}, u32[]{:S(2)}) async-start(f32[16,128,256]{1,2,0:T(8,128)} %copy.78), calls=%async_computation | async-start | bytes 4194304 | tf_op jit(solution)/shard_map/all_to_all | solution.py:175
  75.0 0.2 copy.76
  75.2 0.9 copy.80
  76.1 46.3 %all-to-all-done = f32[16,128,256]{1,2,0:T(8,128)S(1)} async-done(((f32[16,128,256]{1,2,0:T(8,128)}), f32[16,128,256]{1,2,0:T(8,128)S(1)}, u32[]{:S(2)}, u32[]{:S(2)}) %all-to-all-start) | async-done | bytes 2097184 | tf_op jit(solution)/shard_map/all_to_all | solution.py:175
  122.5 0.7 copy.82
  123.2 0.7 copy.81
  (60 shorter events, 1.3 us)
Async XLA Ops:
  0.6 4.1 %copy-start.1 = (bf16[128,128]{1,0:T(8,128)(2,1)S(1)}, bf16[128,128]{1,0:T(8,128)(2,1)}, u32[]{:S(2)}) copy-start(bf16[128,128]{1,0:T(8,128)(2,1)} %param.52) | copy-start | bytes 98308
  0.6 21.2 %copy-start.2 = (bf16[128,128]{1,0:T(8,128)(2,1)S(1)}, bf16[128,128]{1,0:T(8,128)(2,1)}, u32[]{:S(2)}) copy-start(bf16[128,128]{1,0:T(8,128)(2,1)} %param.53) | copy-start | bytes 98308
  58.9 2.9 %copy-start = (f32[128,6]{0,1:T(8,128)}, f32[128,6]{0,1:T(8,128)S(1)}, u32[]{:S(2)}) copy-start(f32[128,6]{0,1:T(8,128)S(1)} %get-tuple-element.1469) | copy-start | bytes 9220
  61.8 60.6 %all-to-all-start = ((f32[16,128,256]{1,2,0:T(8,128)}), f32[16,128,256]{1,2,0:T(8,128)S(1)}, u32[]{:S(2)}, u32[]{:S(2)}) async-start(f32[16,128,256]{1,2,0:T(8,128)} %copy.78), calls=%async_computation | async-start | bytes 4194304 | tf_op jit(solution)/shard_map/all_to_all | solution.py:175
where the time goes:
time: 124 us
  waiting for transfers between devices  46.3 us (37%)
  blocking collectives  39.9 us (32%)
  starting transfers between devices  13.2 us (11%)
  local copies, waits for them, and re-layouts  13.1 us (11%)
  matrix products  5.79 us (5%)
  other arithmetic  4.14 us (3%)
    all_to_all x1, waiting for transfers between devices, body(): lax.all_to_all(partial_sums.reshape(ctx_count, tok_rows, 2 * head_dim), '...  46.3 us
    all_gather x1, blocking collectives, body(): value_piece = lax.all_gather(value_rows, 'ctx', axis=0, tiled=True)  22.8 us
    all_gather x1, blocking collectives, body(): key_piece = lax.all_gather(key_rows, 'ctx', axis=0, tiled=True)  17.1 us
    all_to_all x1, starting transfers between devices, body(): lax.all_to_all(partial_sums.reshape(ctx_count, tok_rows, 2 * head_dim), '...  13.2 us
    dynamic_update_slice x8, local copies, waits for them, and re-layouts, backward_step(): lax.dynamic_update_slice_in_dim(partial_sums, block_sums, key_start, 0)  4.17 us
    unnamed x12, local copies, waits for them, and re-layouts  3.83 us
    reshape x1, local copies, waits for them, and re-layouts, body(): partial_sums.reshape(ctx_count, tok_rows, 2 * head_dim)  2.89 us
  transfers between devices with their start and end apart: 1, of which 1 were waited for; matrix products, arithmetic and copies ran while one was open for 1% of the time, Pallas kernels for 0%

commit v1 on v0

--- a/solution.py
+++ b/solution.py
@@ -93,7 +93,21 @@
     row_peak = jnp.full((tok_rows, head_count), -1e30, jnp.float32)
     row_total = jnp.zeros((tok_rows, head_count), jnp.float32)
     weighted = jnp.zeros((tok_rows, head_count), jnp.float32)
-    key_piece = lax.all_gather(key_rows, "ctx", axis=0, tiled=True)
+    ways, here, step = (lax.axis_size("ctx"), lax.axis_index("ctx"), key_rows.shape[0])
+    shape = [n * ways if d == 0 else n for d, n in enumerate(key_rows.shape)]
+    full = lax.dynamic_update_slice_in_dim(
+        jnp.zeros(shape, key_rows.dtype), key_rows, here * step, axis=0
+    )
+    going_up = going_down = key_rows
+    for far in range(1, ways // 2 + 1):
+        going_up = lax.ppermute(going_up, "ctx", [(d, (d + 1) % ways) for d in range(ways)])
+        full = lax.dynamic_update_slice_in_dim(full, going_up, (here - far) % ways * step, axis=0)
+        if 2 * far < ways:
+            going_down = lax.ppermute(going_down, "ctx", [(d, (d - 1) % ways) for d in range(ways)])
+            full = lax.dynamic_update_slice_in_dim(
+                full, going_down, (here + far) % ways * step, axis=0
+            )
+    key_piece = full
     value_piece = lax.all_gather(value_rows, "ctx", axis=0, tiled=True)
     piece_rows = key_piece.shape[0]
     block_rows = math.gcd(piece_rows, 512)

time: 124 us -> 147 us (1.19)
  starting transfers between devices: 13.2 us -> 47.8 us
  blocking collectives: 39.9 us -> 18.4 us
  waiting for transfers between devices: 46.3 us -> 56 us
    ppermute x0 -> x15, starting transfers between devices: none -> 22.1 us  [the longest x8 21.2 us: body(): lax.ppermute(going_up, 'ctx', [(d, (d + 1) % ways) for d in range(ways)])]
    all_gather x1 -> x0, blocking collectives: 17.1 us -> none  [body(): key_piece = lax.all_gather(key_rows, 'ctx', axis=0, tiled=True)]
    all_to_all x1, starting transfers between devices: 13.2 us -> 25.6 us  [body(): lax.all_to_all(partial_sums.reshape(ctx_count, tok_rows, 2 * head_dim), '...]
    ppermute x0 -> x15, waiting for transfers between devices: none -> 9.67 us  [the longest x7 7.66 us: body(): lax.ppermute(going_down, 'ctx', [(d, (d - 1) % ways) for d in range(ways)])]
    all_gather x1, blocking collectives: 22.8 us -> 18.4 us  [body(): value_piece = lax.all_gather(value_rows, 'ctx', axis=0, tiled=True)]
    unnamed x12 -> x10, local copies, waits for them, and re-layouts: 3.83 us -> 2.89 us
  transfers between devices with their start and end apart: 1 -> 16, of which waited for: 1 -> 8; matrix products, arithmetic and copies ran while one was open for 1% -> 4% of each run, Pallas kernels for 0% -> 0%
where the time goes in v1:
time: 147 us
  waiting for transfers between devices  56 us (38%)
  starting transfers between devices  47.8 us (33%)
  blocking collectives  18.4 us (13%)
  local copies, waits for them, and re-layouts  13.1 us (9%)
  matrix products  5.79 us (4%)
  other arithmetic  4.13 us (3%)
    all_to_all x1, waiting for transfers between devices, body(): lax.all_to_all(partial_sums.reshape(ctx_count, tok_rows, 2 * head_dim), '...  46.3 us
    all_to_all x1, starting transfers between devices, body(): lax.all_to_all(partial_sums.reshape(ctx_count, tok_rows, 2 * head_dim), '...  25.6 us
    ppermute x8, starting transfers between devices, body(): lax.ppermute(going_up, 'ctx', [(d, (d + 1) % ways) for d in range(ways)])  21.2 us
    all_gather x1, blocking collectives, body(): value_piece = lax.all_gather(value_rows, 'ctx', axis=0, tiled=True)  18.4 us
    ppermute x7, waiting for transfers between devices, body(): lax.ppermute(going_down, 'ctx', [(d, (d - 1) % ways) for d in range(ways)])  7.66 us
    dynamic_update_slice x8, local copies, waits for them, and re-layouts, backward_step(): lax.dynamic_update_slice_in_dim(partial_sums, block_sums, key_start, 0)  4.15 us
  transfers between devices with their start and end apart: 16, of which 8 were waited for; matrix products, arithmetic and copies ran while one was open for 4% of the time, Pallas kernels for 0%

profile of v1, /device:TPU:13, one launch (start us, length us, event | category | flops | bytes accessed | tf_op | source)
XLA Modules:
  0.0 147.1 jit_solution(10030525620119498611)
XLA Ops:
  0.6 0.7 collective-permute-start.1
  1.4 2.0 %collective-permute-start = (bf16[128,128]{1,0:T(8,128)(2,1)}, bf16[128,128]{1,0:T(8,128)(2,1)S(1)}, u32[]{:S(2)}, u32[]{:S(2)}) collective-permute-start(bf16[128,128]{1,0:T(8,128)(2,1)} %param.52), channel_id=1, source_target_pairs={{0,2},{2,4},{4,6},{6,8},{8,10},{10,12},{12,14},{14,16},{16,18},{18... | collective-permute-start | bytes 98312 | tf_op jit(solution)/shard_map/ppermute | solution.py:103
  3.3 18.4 %all_gather.3 = bf16[2048,128]{1,0:T(8,128)(2,1)S(1)} all-gather(bf16[128,128]{1,0:T(8,128)(2,1)} %param.53), channel_id=1, replica_groups=mesh['ctx'=16,'head'=2] {'ctx'}, dimensions={0}, use_global_device_ids=true | all-gather | bytes 557056 | tf_op jit(solution)/shard_map/all_gather | solution.py:111
  21.8 0.7 fusion.61
  22.4 0.7 select_reduce_fusion.3
  23.2 1.0 multiply_convert_fusion.1
  24.3 0.8 constant_dynamic-update-slice_fusion.16
  26.4 2.5 %collective-permute-start.2 = (bf16[128,128]{1,0:T(8,128)(2,1)S(1)}, bf16[128,128]{1,0:T(8,128)(2,1)S(1)}, u32[]{:S(2)}, u32[]{:S(2)}) collective-permute-start(bf16[128,128]{1,0:T(8,128)(2,1)S(1)} %collective-permute-done), channel_id=1, source_target_pairs={{0,2},{2,4},{4,6},{6,8},{8,10},{10,12},{12,14},{14,16},{16,18},{18... | collective-permute-start | bytes 98312 | tf_op jit(solution)/shard_map/ppermute | solution.py:103
  28.9 1.6 %collective-permute-done.3 = bf16[128,128]{1,0:T(8,128)(2,1)S(1)} collective-permute-done((bf16[128,128]{1,0:T(8,128)(2,1)S(1)}, bf16[128,128]{1,0:T(8,128)(2,1)S(1)}, u32[]{:S(2)}, u32[]{:S(2)}) %collective-permute-start.3) | collective-permute-done | bytes 32800 | tf_op jit(solution)/shard_map/ppermute | solution.py:106
  30.5 2.7 %collective-permute-start.4 = (bf16[128,128]{1,0:T(8,128)(2,1)S(1)}, bf16[128,128]{1,0:T(8,128)(2,1)S(1)}, u32[]{:S(2)}, u32[]{:S(2)}) collective-permute-start(bf16[128,128]{1,0:T(8,128)(2,1)S(1)} %collective-permute-done.2), channel_id=1, source_target_pairs={{0,2},{2,4},{4,6},{6,8},{8,10},{10,12},{12,14},{14,16},{16,18},{18... | collective-permute-start | bytes 98312 | tf_op jit(solution)/shard_map/ppermute | solution.py:103
  33.2 1.5 %collective-permute-done.5 = bf16[128,128]{1,0:T(8,128)(2,1)S(1)} collective-permute-done((bf16[128,128]{1,0:T(8,128)(2,1)S(1)}, bf16[128,128]{1,0:T(8,128)(2,1)S(1)}, u32[]{:S(2)}, u32[]{:S(2)}) %collective-permute-start.5) | collective-permute-done | bytes 32800 | tf_op jit(solution)/shard_map/ppermute | solution.py:106
  34.7 2.7 %collective-permute-start.6 = (bf16[128,128]{1,0:T(8,128)(2,1)S(1)}, bf16[128,128]{1,0:T(8,128)(2,1)S(1)}, u32[]{:S(2)}, u32[]{:S(2)}) collective-permute-start(bf16[128,128]{1,0:T(8,128)(2,1)S(1)} %collective-permute-done.4), channel_id=1, source_target_pairs={{0,2},{2,4},{4,6},{6,8},{8,10},{10,12},{12,14},{14,16},{16,18},{18... | collective-permute-start | bytes 98312 | tf_op jit(solution)/shard_map/ppermute | solution.py:103
  37.4 1.5 %collective-permute-done.7 = bf16[128,128]{1,0:T(8,128)(2,1)S(1)} collective-permute-done((bf16[128,128]{1,0:T(8,128)(2,1)S(1)}, bf16[128,128]{1,0:T(8,128)(2,1)S(1)}, u32[]{:S(2)}, u32[]{:S(2)}) %collective-permute-start.7) | collective-permute-done | bytes 32800 | tf_op jit(solution)/shard_map/ppermute | solution.py:106
  39.0 2.7 %collective-permute-start.8 = (bf16[128,128]{1,0:T(8,128)(2,1)S(1)}, bf16[128,128]{1,0:T(8,128)(2,1)S(1)}, u32[]{:S(2)}, u32[]{:S(2)}) collective-permute-start(bf16[128,128]{1,0:T(8,128)(2,1)S(1)} %collective-permute-done.6), channel_id=1, source_target_pairs={{0,2},{2,4},{4,6},{6,8},{8,10},{10,12},{12,14},{14,16},{16,18},{18... | collective-permute-start | bytes 98312 | tf_op jit(solution)/shard_map/ppermute | solution.py:103
  41.7 1.5 %collective-permute-done.9 = bf16[128,128]{1,0:T(8,128)(2,1)S(1)} collective-permute-done((bf16[128,128]{1,0:T(8,128)(2,1)S(1)}, bf16[128,128]{1,0:T(8,128)(2,1)S(1)}, u32[]{:S(2)}, u32[]{:S(2)}) %collective-permute-start.9) | collective-permute-done | bytes 32800 | tf_op jit(solution)/shard_map/ppermute | solution.py:106
  43.2 2.7 %collective-permute-start.10 = (bf16[128,128]{1,0:T(8,128)(2,1)S(1)}, bf16[128,128]{1,0:T(8,128)(2,1)S(1)}, u32[]{:S(2)}, u32[]{:S(2)}) collective-permute-start(bf16[128,128]{1,0:T(8,128)(2,1)S(1)} %collective-permute-done.8), channel_id=1, source_target_pairs={{0,2},{2,4},{4,6},{6,8},{8,10},{10,12},{12,14},{14,16},{16,18},{18... | collective-permute-start | bytes 98312 | tf_op jit(solution)/shard_map/ppermute | solution.py:103
  45.9 1.5 %collective-permute-done.11 = bf16[128,128]{1,0:T(8,128)(2,1)S(1)} collective-permute-done((bf16[128,128]{1,0:T(8,128)(2,1)S(1)}, bf16[128,128]{1,0:T(8,128)(2,1)S(1)}, u32[]{:S(2)}, u32[]{:S(2)}) %collective-permute-start.11) | collective-permute-done | bytes 32800 | tf_op jit(solution)/shard_map/ppermute | solution.py:106
  47.4 2.7 %collective-permute-start.12 = (bf16[128,128]{1,0:T(8,128)(2,1)S(1)}, bf16[128,128]{1,0:T(8,128)(2,1)S(1)}, u32[]{:S(2)}, u32[]{:S(2)}) collective-permute-start(bf16[128,128]{1,0:T(8,128)(2,1)S(1)} %collective-permute-done.10), channel_id=1, source_target_pairs={{0,2},{2,4},{4,6},{6,8},{8,10},{10,12},{12,14},{14,16},{16,18},{18... | collective-permute-start | bytes 98312 | tf_op jit(solution)/shard_map/ppermute | solution.py:103
  50.2 1.0 collective-permute-done.12
  51.2 3.2 %collective-permute-start.14 = (bf16[128,128]{1,0:T(8,128)(2,1)S(1)}, bf16[128,128]{1,0:T(8,128)(2,1)S(1)}, u32[]{:S(2)}, u32[]{:S(2)}) collective-permute-start(bf16[128,128]{1,0:T(8,128)(2,1)S(1)} %collective-permute-done.12), channel_id=1, source_target_pairs={{0,2},{2,4},{4,6},{6,8},{8,10},{10,12},{12,14},{14,16},{16,18},{18... | collective-permute-start | bytes 98312 | tf_op jit(solution)/shard_map/ppermute | solution.py:103
  54.4 1.0 collective-permute-done.14
  55.4 3.9 %while.53 = (s32[]{:T(128)}, f32[128,6]{0,1:T(8,128)S(1)}, f32[128,6]{0,1:T(8,128)S(1)}, f32[128,6]{0,1:T(8,128)S(1)}, s32[]{:T(128)}, /*index=5*/s32[]{:T(128)}...) while((s32[]{:T(128)}, f32[128,6]{0,1:T(8,128)S(1)}, ...), condition=%wide.region_15.16_spmd.clone, body=%wide.region_1.15_spmd.clone.sunk | while | flops 205327120 | bytes 6221379 | solution.py:121
  55.5 1.7 %conditional.6 = ((f32[128,6]{0,1:T(8,128)S(1)}, f32[128,6]{0,1:T(8,128)S(1)}, f32[128,6]{0,1:T(8,128)S(1)})) conditional(s32[]{:T(128)} %clamp.18, (f32[128,6]{0,1:T(8,128)S(1)}, f32[128,6]{0,1:T(8,128)S(1)}, f32[128,6]{0,1:T(8,128)S(1)}) %tuple.202, (f32[128,6]{0,1:T(8,128)S(1)}, s32[]{:T(128)}, s32[]{:T(128)}, ...), branch_computations={%region_2.2_spmd, %region_3.6_spmd, %region_7.0_spmd, %region_11.0... | conditional | flops 205327104 | bytes 5696036 | solution.py:61
  55.7 0.5 select_reduce_fusion.2
  56.2 0.6 multiply_reduce_fusion
  56.7 0.5 fusion.20
  57.3 1.7 %conditional.6 = ((f32[128,6]{0,1:T(8,128)S(1)}, f32[128,6]{0,1:T(8,128)S(1)}, f32[128,6]{0,1:T(8,128)S(1)})) conditional(s32[]{:T(128)} %clamp.18, (f32[128,6]{0,1:T(8,128)S(1)}, f32[128,6]{0,1:T(8,128)S(1)}, f32[128,6]{0,1:T(8,128)S(1)}) %tuple.202, (f32[128,6]{0,1:T(8,128)S(1)}, s32[]{:T(128)}, s32[]{:T(128)}, ...), branch_computations={%region_2.2_spmd, %region_3.6_spmd, %region_7.0_spmd, %region_11.0... | conditional | flops 205327104 | bytes 5696036 | solution.py:61
  57.5 0.5 select_reduce_fusion.2
  58.0 0.6 multiply_reduce_fusion
  58.5 0.5 fusion.20
  59.4 1.5 %broadcast_in_dim.128.clone = f32[2048,256]{1,0:T(8,128)} broadcast(f32[]{:T(128)} %constant.571.clone.1), dimensions={} | broadcast | bytes 2097156 | tf_op jit(solution)/shard_map/broadcast_in_dim | solution.py:186
  60.9 8.7 %while.54 = (s32[]{:T(128)}, f32[128,6,128]{2,0,1:T(8,128)S(1)}, f32[2048,256]{1,0:T(8,128)}, s32[]{:T(128)}, s32[]{:T(128)}, /*index=5*/bf16[2048,128]{1,0:T(8,...) while((s32[]{:T(128)}, f32[128,6,128]{2,0,1:T(8,128)S(1)}, ...), condition=%wide.region_21.22_spmd.clone, body=%wide.region_16.21_spmd.clone.sunk | while | flops 506528256 | bytes 13381159 | solution.py:182
  60.9 2.1 %conditional.7 = (f32[128,6,128]{2,0,1:T(8,128)S(1)}, f32[512,256]{0,1:T(8,128)S(1)}) conditional(s32[]{:T(128)} %clamp.19, f32[128,6,128]{2,0,1:T(8,128)S(1)} %get-tuple-element.1421, (f32[128,6,128]{2,0,1:T(8,128)S(1)}, s32[]{:T(128)}, s32[]{:T(128)}, bf16[128,6,128]{0,2,1:T(8,128)(2,1)S(1)}, ...), branch_computations={%region_17.17_spmd, %region_18.18_spmd, %region_19.19_spmd, %regio... | conditional | flops 506528256 | bytes 10758676 | solution.py:61
  61.1 0.5 exponential_select_fusion.3
  61.9 0.4 multiply_convert_fusion
  63.2 0.8 constant_dynamic-update-slice_fusion.18
  64.1 2.1 %conditional.7 = (f32[128,6,128]{2,0,1:T(8,128)S(1)}, f32[512,256]{0,1:T(8,128)S(1)}) conditional(s32[]{:T(128)} %clamp.19, f32[128,6,128]{2,0,1:T(8,128)S(1)} %get-tuple-element.1421, (f32[128,6,128]{2,0,1:T(8,128)S(1)}, s32[]{:T(128)}, s32[]{:T(128)}, bf16[128,6,128]{0,2,1:T(8,128)(2,1)S(1)}, ...), branch_computations={%region_17.17_spmd, %region_18.18_spmd, %region_19.19_spmd, %regio... | conditional | flops 506528256 | bytes 10758676 | solution.py:61
  64.2 0.5 exponential_select_fusion.3
  65.1 0.4 multiply_convert_fusion
  66.4 0.8 constant_dynamic-update-slice_fusion.18
  67.6 0.8 constant_dynamic-update-slice_fusion.18
  68.8 0.8 constant_dynamic-update-slice_fusion.18
  69.6 2.9 %copy.78 = f32[16,128,256]{1,2,0:T(8,128)} copy(f32[16,128,256]{2,1,0:T(8,128)} %bitcast.88) | data formatting | bytes 4194304 | tf_op jit(solution)/shard_map/reshape | solution.py:190
  72.5 25.6 %all-to-all-start = ((f32[16,128,256]{1,2,0:T(8,128)}), f32[16,128,256]{1,2,0:T(8,128)S(1)}, u32[]{:S(2)}, u32[]{:S(2)}) async-start(f32[16,128,256]{1,2,0:T(8,128)} %copy.78), calls=%async_computation | async-start | bytes 4194304 | tf_op jit(solution)/shard_map/all_to_all | solution.py:189
  98.3 0.9 copy.80
  99.2 46.3 %all-to-all-done = f32[16,128,256]{1,2,0:T(8,128)S(1)} async-done(((f32[16,128,256]{1,2,0:T(8,128)}), f32[16,128,256]{1,2,0:T(8,128)S(1)}, u32[]{:S(2)}, u32[]{:S(2)}) %all-to-all-start) | async-done | bytes 2097184 | tf_op jit(solution)/shard_map/all_to_all | solution.py:189
  145.6 0.7 copy.82
  146.4 0.7 copy.81
  (104 shorter events, 5.3 us)
Async XLA Ops:
  0.6 25.1 %copy-start = (bf16[128,768]{1,0:T(8,128)(2,1)S(1)}, bf16[128,768]{1,0:T(8,128)(2,1)}, u32[]{:S(2)}) copy-start(bf16[128,768]{1,0:T(8,128)(2,1)} %param.51) | copy-start | bytes 589828
  0.6 25.5 %collective-permute-start.1 = (bf16[128,128]{1,0:T(8,128)(2,1)}, bf16[128,128]{1,0:T(8,128)(2,1)S(1)}, u32[]{:S(2)}, u32[]{:S(2)}) collective-permute-start(bf16[128,128]{1,0:T(8,128)(2,1)} %param.52), channel_id=1, source_target_pairs={{0,30},{2,0},{4,2},{6,4},{8,6},{10,8},{12,10},{14,12},{16,14},{18,... | collective-permute-start | bytes 98312 | tf_op jit(solution)/shard_map/ppermute | solution.py:106
  1.4 25.0 %collective-permute-start = (bf16[128,128]{1,0:T(8,128)(2,1)}, bf16[128,128]{1,0:T(8,128)(2,1)S(1)}, u32[]{:S(2)}, u32[]{:S(2)}) collective-permute-start(bf16[128,128]{1,0:T(8,128)(2,1)} %param.52), channel_id=1, source_target_pairs={{0,2},{2,4},{4,6},{6,8},{8,10},{10,12},{12,14},{14,16},{16,18},{18... | collective-permute-start | bytes 98312 | tf_op jit(solution)/shard_map/ppermute | solution.py:103
  26.1 4.3 %collective-permute-start.3 = (bf16[128,128]{1,0:T(8,128)(2,1)S(1)}, bf16[128,128]{1,0:T(8,128)(2,1)S(1)}, u32[]{:S(2)}, u32[]{:S(2)}) collective-permute-start(bf16[128,128]{1,0:T(8,128)(2,1)S(1)} %collective-permute-done.1), channel_id=1, source_target_pairs={{0,30},{2,0},{4,2},{6,4},{8,6},{10,8},{12,10},{14,12},{16,14},{18,... | collective-permute-start | bytes 98312 | tf_op jit(solution)/shard_map/ppermute | solution.py:106
  26.4 4.1 %collective-permute-start.2 = (bf16[128,128]{1,0:T(8,128)(2,1)S(1)}, bf16[128,128]{1,0:T(8,128)(2,1)S(1)}, u32[]{:S(2)}, u32[]{:S(2)}) collective-permute-start(bf16[128,128]{1,0:T(8,128)(2,1)S(1)} %collective-permute-done), channel_id=1, source_target_pairs={{0,2},{2,4},{4,6},{6,8},{8,10},{10,12},{12,14},{14,16},{16,18},{18... | collective-permute-start | bytes 98312 | tf_op jit(solution)/shard_map/ppermute | solution.py:103
  30.5 4.2 %collective-permute-start.5 = (bf16[128,128]{1,0:T(8,128)(2,1)S(1)}, bf16[128,128]{1,0:T(8,128)(2,1)S(1)}, u32[]{:S(2)}, u32[]{:S(2)}) collective-permute-start(bf16[128,128]{1,0:T(8,128)(2,1)S(1)} %collective-permute-done.3), channel_id=1, source_target_pairs={{0,30},{2,0},{4,2},{6,4},{8,6},{10,8},{12,10},{14,12},{16,14},{18,... | collective-permute-start | bytes 98312 | tf_op jit(solution)/shard_map/ppermute | solution.py:106
  30.5 4.2 %collective-permute-start.4 = (bf16[128,128]{1,0:T(8,128)(2,1)S(1)}, bf16[128,128]{1,0:T(8,128)(2,1)S(1)}, u32[]{:S(2)}, u32[]{:S(2)}) collective-permute-start(bf16[128,128]{1,0:T(8,128)(2,1)S(1)} %collective-permute-done.2), channel_id=1, source_target_pairs={{0,2},{2,4},{4,6},{6,8},{8,10},{10,12},{12,14},{14,16},{16,18},{18... | collective-permute-start | bytes 98312 | tf_op jit(solution)/shard_map/ppermute | solution.py:103
  34.7 4.2 %collective-permute-start.7 = (bf16[128,128]{1,0:T(8,128)(2,1)S(1)}, bf16[128,128]{1,0:T(8,128)(2,1)S(1)}, u32[]{:S(2)}, u32[]{:S(2)}) collective-permute-start(bf16[128,128]{1,0:T(8,128)(2,1)S(1)} %collective-permute-done.5), channel_id=1, source_target_pairs={{0,30},{2,0},{4,2},{6,4},{8,6},{10,8},{12,10},{14,12},{16,14},{18,... | collective-permute-start | bytes 98312 | tf_op jit(solution)/shard_map/ppermute | solution.py:106
  34.7 4.2 %collective-permute-start.6 = (bf16[128,128]{1,0:T(8,128)(2,1)S(1)}, bf16[128,128]{1,0:T(8,128)(2,1)S(1)}, u32[]{:S(2)}, u32[]{:S(2)}) collective-permute-start(bf16[128,128]{1,0:T(8,128)(2,1)S(1)} %collective-permute-done.4), channel_id=1, source_target_pairs={{0,2},{2,4},{4,6},{6,8},{8,10},{10,12},{12,14},{14,16},{16,18},{18... | collective-permute-start | bytes 98312 | tf_op jit(solution)/shard_map/ppermute | solution.py:103
  39.0 4.2 %collective-permute-start.9 = (bf16[128,128]{1,0:T(8,128)(2,1)S(1)}, bf16[128,128]{1,0:T(8,128)(2,1)S(1)}, u32[]{:S(2)}, u32[]{:S(2)}) collective-permute-start(bf16[128,128]{1,0:T(8,128)(2,1)S(1)} %collective-permute-done.7), channel_id=1, source_target_pairs={{0,30},{2,0},{4,2},{6,4},{8,6},{10,8},{12,10},{14,12},{16,14},{18,... | collective-permute-start | bytes 98312 | tf_op jit(solution)/shard_map/ppermute | solution.py:106
  39.0 4.2 %collective-permute-start.8 = (bf16[128,128]{1,0:T(8,128)(2,1)S(1)}, bf16[128,128]{1,0:T(8,128)(2,1)S(1)}, u32[]{:S(2)}, u32[]{:S(2)}) collective-permute-start(bf16[128,128]{1,0:T(8,128)(2,1)S(1)} %collective-permute-done.6), channel_id=1, source_target_pairs={{0,2},{2,4},{4,6},{6,8},{8,10},{10,12},{12,14},{14,16},{16,18},{18... | collective-permute-start | bytes 98312 | tf_op jit(solution)/shard_map/ppermute | solution.py:103
  43.2 4.2 %collective-permute-start.11 = (bf16[128,128]{1,0:T(8,128)(2,1)S(1)}, bf16[128,128]{1,0:T(8,128)(2,1)S(1)}, u32[]{:S(2)}, u32[]{:S(2)}) collective-permute-start(bf16[128,128]{1,0:T(8,128)(2,1)S(1)} %collective-permute-done.9), channel_id=1, source_target_pairs={{0,30},{2,0},{4,2},{6,4},{8,6},{10,8},{12,10},{14,12},{16,14},{18,... | collective-permute-start | bytes 98312 | tf_op jit(solution)/shard_map/ppermute | solution.py:106
  43.2 4.2 %collective-permute-start.10 = (bf16[128,128]{1,0:T(8,128)(2,1)S(1)}, bf16[128,128]{1,0:T(8,128)(2,1)S(1)}, u32[]{:S(2)}, u32[]{:S(2)}) collective-permute-start(bf16[128,128]{1,0:T(8,128)(2,1)S(1)} %collective-permute-done.8), channel_id=1, source_target_pairs={{0,2},{2,4},{4,6},{6,8},{8,10},{10,12},{12,14},{14,16},{16,18},{18... | collective-permute-start | bytes 98312 | tf_op jit(solution)/shard_map/ppermute | solution.py:103
  47.4 7.0 %collective-permute-start.13 = (bf16[128,128]{1,0:T(8,128)(2,1)S(1)}, bf16[128,128]{1,0:T(8,128)(2,1)S(1)}, u32[]{:S(2)}, u32[]{:S(2)}) collective-permute-start(bf16[128,128]{1,0:T(8,128)(2,1)S(1)} %collective-permute-done.11), channel_id=1, source_target_pairs={{0,30},{2,0},{4,2},{6,4},{8,6},{10,8},{12,10},{14,12},{16,14},{18,... | collective-permute-start | bytes 98312 | tf_op jit(solution)/shard_map/ppermute | solution.py:106
  47.4 3.7 %collective-permute-start.12 = (bf16[128,128]{1,0:T(8,128)(2,1)S(1)}, bf16[128,128]{1,0:T(8,128)(2,1)S(1)}, u32[]{:S(2)}, u32[]{:S(2)}) collective-permute-start(bf16[128,128]{1,0:T(8,128)(2,1)S(1)} %collective-permute-done.10), channel_id=1, source_target_pairs={{0,2},{2,4},{4,6},{6,8},{8,10},{10,12},{12,14},{14,16},{16,18},{18... | collective-permute-start | bytes 98312 | tf_op jit(solution)/shard_map/ppermute | solution.py:103
  51.2 4.2 %collective-permute-start.14 = (bf16[128,128]{1,0:T(8,128)(2,1)S(1)}, bf16[128,128]{1,0:T(8,128)(2,1)S(1)}, u32[]{:S(2)}, u32[]{:S(2)}) collective-permute-start(bf16[128,128]{1,0:T(8,128)(2,1)S(1)} %collective-permute-done.12), channel_id=1, source_target_pairs={{0,2},{2,4},{4,6},{6,8},{8,10},{10,12},{12,14},{14,16},{16,18},{18... | collective-permute-start | bytes 98312 | tf_op jit(solution)/shard_map/ppermute | solution.py:103
  69.6 2.9 %copy-start.1 = (f32[128,6]{0,1:T(8,128)}, f32[128,6]{0,1:T(8,128)S(1)}, u32[]{:S(2)}) copy-start(f32[128,6]{0,1:T(8,128)S(1)} %get-tuple-element.1469) | copy-start | bytes 9220
  72.5 73.0 %all-to-all-start = ((f32[16,128,256]{1,2,0:T(8,128)}), f32[16,128,256]{1,2,0:T(8,128)S(1)}, u32[]{:S(2)}, u32[]{:S(2)}) async-start(f32[16,128,256]{1,2,0:T(8,128)} %copy.78), calls=%async_computation | async-start | bytes 4194304 | tf_op jit(solution)/shard_map/all_to_all | solution.py:189
